TPU v7x, 256 devices: a whole 4x4x8 slice. The times are simulated.
256 devices in a mesh: day: 8 (over x, core), row: 32 (over y, z).
Axes of the slice: x: 4, y: 4, z: 8, core: 2. Of those that a mesh axis runs over, the one named last changes fastest.
Arguments:
- features: bfloat16 [8, 768, 16, 128, 128], P('day', 'row'), may hold values from -6 to 6
- blocks: int32 [8, 768, 16], P('day', 'row'), may hold values from 0 to 255, as said below
- labels: int32 [8, 768, 128], P('day', 'row'), may hold values from 0 to 15
- coef: float32 [8, 16, 32768], P('day', None, 'row'), may hold values from -0.125 to 0.125
- direction: float32 [8, 16, 32768], P('day', None, 'row'), may hold values from -0.125 to 0.125
- prior: float32 [32768], P('row'), may hold values from 100 to 3000
Outputs:
- gradient: float32 [8, 16, 32768], P('day', None, 'row')
- hess_dir: float32 [8, 16, 32768], P('day', None, 'row')
Inputs may be any that keep to these rules, and one draw needn't show every extreme that they name: `blocks`: within one row tile the 16 block numbers are distinct.
All inputs are finite; a program needn't handle non-finite values.
Results may differ from a plain program's by a relative error of at most 0.0003.
Values may be sent and summed in bfloat16 or wider, within the bound.
No kernel may reach another device: no remote copies, remote signals or barrier semaphores. Data moves between devices by JAX's collectives and lax.ppermute only.
A program may use at most 64 MiB of HBM per device.

v0:
```python
import jax
import jax.numpy as jnp
from jax import lax
from jax.sharding import Mesh
from jax.sharding import PartitionSpec as P

ROW = ("row_0", "row_1")


def extended(cells, sides, width):
    for axis, dim in sides:
        count = lax.axis_size(axis)
        ends = count - 1
        head = lax.slice_in_dim(cells, 0, width, axis=dim)
        tail = lax.slice_in_dim(cells, cells.shape[dim] - width, cells.shape[dim], axis=dim)
        cells = jnp.concatenate(
            [
                lax.ppermute(tail, axis, [(i, (i + 1) % count) for i in range(ends)]),
                cells,
                lax.ppermute(head, axis, [((i + 1) % count, i) for i in range(ends)]),
            ],
            axis=dim,
        )
    return cells


def on_device(features, blocks, labels, coef, direction, prior):
    arms = coef.shape[1]
    width = features.shape[-1]
    coef_pair = jnp.concatenate([coef[0], direction[0]], axis=0).astype(jnp.bfloat16)
    coef_table = lax.all_gather(coef_pair, ROW, axis=1, tiled=True)
    nfeat = coef_table.shape[1]
    nblk = nfeat // width
    both = jnp.concatenate([coef, direction], axis=1)
    neighbours = extended(both, (("day", 0),), 1)
    blks = blocks[0]
    selected = coef_table.reshape(2 * arms, nblk, width)[:, blks]
    feats = features[0]
    logits_dir = jnp.einsum("tari,ktai->tkr", feats, selected, preferred_element_type=jnp.float32)
    logits = logits_dir[:, :arms]
    lin_dir = logits_dir[:, arms:]
    expo = jnp.exp(logits)
    probs = expo / jnp.sum(expo, axis=1, keepdims=True)
    onehot = (labels[0][:, None, :] == jnp.arange(arms, dtype=jnp.int32)[None, :, None]).astype(
        jnp.float32
    )
    resid = probs - onehot
    hrow = probs * lin_dir - probs * jnp.sum(probs * lin_dir, axis=1, keepdims=True)
    both_low = jnp.concatenate([resid, hrow], axis=1).astype(jnp.bfloat16)
    contrib = jnp.einsum("tari,tkr->taki", feats, both_low, preferred_element_type=jnp.float32)
    contrib = contrib.reshape(-1, 2 * arms, width)
    top = lax.reduce_precision(contrib, exponent_bits=8, mantissa_bits=7)
    hi = top.astype(jnp.bfloat16)
    lo = (contrib - top).astype(jnp.bfloat16)
    place = (blks.reshape(-1)[:, None] == jnp.arange(nblk, dtype=jnp.int32)[None, :]).astype(
        jnp.bfloat16
    )
    parts = jnp.einsum(
        "pb,pjki->jkbi", place, jnp.stack([hi, lo], axis=1), preferred_element_type=jnp.float32
    )
    partial_terms = parts[0] + parts[1]
    partial_terms = partial_terms.reshape(2 * arms, nfeat)
    owned = lax.psum_scatter(partial_terms, ROW, scatter_dimension=1, tiled=True)
    day_index = lax.axis_index("day")
    ndays = lax.axis_size("day")
    links = (day_index > 0).astype(jnp.float32) + (day_index < ndays - 1).astype(jnp.float32)
    coupling = links * neighbours[1] - neighbours[0] - neighbours[2]
    result = owned + prior[None, :] * coupling
    return (result[None, :arms], result[None, arms:])


def solution(mesh):
    finer = Mesh(mesh.devices.reshape(mesh.shape["day"], 4, 8), ("day", "row_0", "row_1"))
    return jax.shard_map(
        on_device,
        mesh=finer,
        in_specs=(
            P("day", ROW, None, None, None),
            P("day", ROW, None),
            P("day", ROW, None),
            P("day", None, ROW),
            P("day", None, ROW),
            P(ROW),
        ),
        out_specs=(P("day", None, ROW), P("day", None, ROW)),
        check_vma=False,
    )
```

profile of v0, /device:TPU:4, one launch (start us, length us, event | category | flops | bytes accessed | tf_op | source)
XLA Modules:
  0.0 374.2 jit_solution(4076354408150905320)
XLA Ops:
  7.2 0.0 all-gather.2.cloned.1.call-start
  7.2 0.9 constant_dynamic-update-slice_fusion.1
  8.1 0.9 constant_dynamic-update-slice_fusion
  9.1 0.6 pad_maximum_fusion
  9.7 0.0 all-gather.2.cloned.1.call-update
  9.7 0.0 reduce-scatter.2.cloned.1.call-start
  9.8 0.8 copy.20
  10.5 0.7 compare_select_fusion
  11.2 0.1 copy.16
  11.3 0.1 reshape.84
  11.4 0.1 eq.34
  11.5 80.7 %all-gather.2.cloned.1.call-done = bf16[32,32768]{1,0:T(8,128)(2,1)} async-done(((bf16[32,1024]{1,0:T(8,128)(2,1)}), bf16[32,32768]{1,0:T(8,128)(2,1)}) %all-gather.2.cloned.1.call-update) | async-done | bytes 2097168 | tf_op jit(solution)/shard_map/all_gather | solution.py:31
  92.2 2.0 copy_bitcast_fusion.1
  94.2 3.2 gather_fusion
  97.3 0.0 copy-start.1
  97.3 9.7 %fusion.14 = f32[24,32,128]{2,1,0:T(8,128)S(1)} fusion(bf16[32,24,16,128]{3,0,2,1:T(8,128)(2,1)} %bitcast.59, bf16[1,24,16,128,128]{4,3,2,1,0:T(8,128)(2,1)} %param.6), kind=kOutput, calls=%fused_computation.18 | convolution fusion | flops 402653184 | bytes 16121856 | tf_op jit(solution)/shard_map/tari,ktai->tkr/dot_general | solution.py:39
  107.0 0.0 copy-done.1
  107.0 0.8 subtract_convert_fusion
  107.8 0.1 fusion.20
  107.9 9.0 %fusion.2 = f32[24,32,16,128]{3,1,2,0:T(8,128)} fusion(bf16[1,24,16,128,128]{4,3,2,1,0:T(8,128)(2,1)} %param.6, bf16[24,16,128]{2,1,0:T(8,128)(2,1)S(1)} %fusion.20, bf16[24,16,128]{2,1,0:T(8,128)(2,1)S(1)} %get-tuple-element.10), kind=kOutput, calls=%fused_computation.3 | convolution fusion | flops 403046400 | bytes 19070976 | tf_op jit(solution)/shard_map/tari,tkr->taki/dot_general | solution.py:50
  116.9 6.6 %copy.18 = f32[384,1,32,128]{0,3,2,1:T(8,128)} copy(f32[384,1,32,128]{3,2,0,1:T(8,128)} %bitcast.56) | data formatting | bytes 12582912 | tf_op jit(solution)/shard_map/reshape | solution.py:51
  123.4 4.3 %reduce-precision_convert_fusion = (bf16[384,1,32,128]{0,3,2,1:T(8,128)(2,1)S(1)}, bf16[384,1,32,128]{0,3,2,1:T(8,128)(2,1)S(1)}) fusion(f32[384,1,32,128]{0,3,2,1:T(8,128)} %copy.18), kind=kLoop, calls=%fused_computation.8 | loop fusion | flops 6291456 | bytes 12582912 | tf_op jit(solution)/shard_map/convert_element_type | solution.py:53
  127.7 2.5 fusion.11
  130.2 2.8 slice_add_fusion
  132.9 5.6 %copy.21 = f32[1,32,256,128]{3,2,1,0:T(8,128)} copy(f32[1,32,256,128]{2,3,1,0:T(8,128)} %slice_add_fusion) | data formatting | bytes 8388608 | tf_op jit(solution)/shard_map/add | solution.py:61
  138.5 6.6 %copy.29 = f32[4,8,256,128]{3,1,2,0:T(8,128)} copy(f32[4,8,256,128]{3,2,1,0:T(8,128)} %bitcast.58) | data formatting | bytes 8388608
  145.1 0.0 copy-start
  145.1 0.0 reduce-scatter.2.cloned.1.call-update
  145.1 1.9 collective-permute-start
  147.0 3.6 collective-permute-start.1
  150.7 0.7 collective-permute-done
  151.4 1.8 collective-permute-done.1
  153.2 212.6 %reduce-scatter.2.cloned.1.call-done = f32[32,1024]{1,0:T(8,128)} async-done(((f32[32,32768]{1,0:T(8,128)}), f32[32,1024]{1,0:T(8,128)}) %reduce-scatter.2.cloned.1.call-update) | async-done | bytes 131088 | tf_op jit(solution)/shard_map/reduce_scatter | solution.py:63
  365.8 0.0 copy-done
  365.8 0.9 fusion.28
  366.7 0.7 slice_bitcast_fusion
  (1 shorter events, 0.0 us)
Async XLA Ops:
  7.2 85.1 %all-gather.2.cloned.1.call-start = ((), (), s32[]{:S(2)}) async-start(), calls=%async_computation.1 | async-start | bytes 2162688 | tf_op jit(solution)/shard_map/all_gather | solution.py:31
  9.7 356.0 %reduce-scatter.2.cloned.1.call-start = ((), (), s32[]{:S(2)}) async-start(), calls=%async_computation.2 | async-start | bytes 4325376 | tf_op jit(solution)/shard_map/reduce_scatter | solution.py:63
  97.3 9.7 %copy-start.1 = (s32[1,24,128]{2,1,0:T(8,128)S(1)}, s32[1,24,128]{2,1,0:T(8,128)}, u32[]{:S(2)}) copy-start(s32[1,24,128]{2,1,0:T(8,128)} %param.8) | copy-start | bytes 36868
  145.1 220.7 %copy-start = (f32[1024]{0:T(1024)S(1)}, f32[1024]{0:T(1024)}, u32[]{:S(2)}) copy-start(f32[1024]{0:T(1024)} %param.11) | copy-start | bytes 12292
  145.1 6.3 %collective-permute-start = (f32[1,32,1024]{2,1,0:T(8,128)S(1)}, f32[1,32,1024]{2,1,0:T(8,128)S(1)}, u32[]{:S(2)}, u32[]{:S(2)}) collective-permute-start(f32[1,32,1024]{2,1,0:T(8,128)S(1)} %get-tuple-element.6), channel_id=1, source_target_pairs={{0,32},{32,64},{64,96},{96,128},{128,160},{160,192},{192,224},{1,3... | collective-permute-start | bytes 393224 | tf_op jit(solution)/shard_map/ppermute | solution.py:18
  147.0 6.1 %collective-permute-start.1 = (f32[1,32,1024]{2,1,0:T(8,128)S(1)}, f32[1,32,1024]{2,1,0:T(8,128)S(1)}, u32[]{:S(2)}, u32[]{:S(2)}) collective-permute-start(f32[1,32,1024]{2,1,0:T(8,128)S(1)} %get-tuple-element.6), channel_id=1, source_target_pairs={{32,0},{64,32},{96,64},{128,96},{160,128},{192,160},{224,192},{33,... | collective-permute-start | bytes 393224 | tf_op jit(solution)/shard_map/ppermute | solution.py:20
Sparse Core Ops, SparseCore 0:
  11.1 81.0 all-gather.1
  145.2 220.4 reduce-scatter.1
where the time goes:
time: 375 us; the launch traced here: 374 us
  waiting for transfers between devices  296 us (79%)
  local copies, waits for them, and re-layouts  25.5 us (7%)
  matrix products  21.1 us (6%)
  between operations  14.1 us (4%)
  other arithmetic  12 us (3%)
  starting transfers between devices  5.64 us (2%)
    reduce_scatter x1, waiting for transfers between devices, on_device(): lax.psum_scatter(partial_terms, ROW, scatter_dimension=1, tiled=True)  213 us
    all_gather x1, waiting for transfers between devices, on_device(): coef_table = lax.all_gather(coef_pair, ROW, axis=1, tiled=True)  80.7 us
    dot_general x1, matrix products, on_device(): jnp.einsum('tari,ktai->tkr', feats, selected, preferred_element_type=jnp....  9.67 us
    dot_general x1, matrix products, on_device(): jnp.einsum('tari,tkr->taki', feats, both_low, preferred_element_type=jnp....  9.02 us
  transfers between devices with their start and end apart: 4, of which 4 were waited for; matrix products, arithmetic and copies ran while one was open for 0% of the time, Pallas kernels for 0%

commit v1 on v0

--- a/solution.py
+++ b/solution.py
@@ -28,7 +28,10 @@
     arms = coef.shape[1]
     width = features.shape[-1]
     coef_pair = jnp.concatenate([coef[0], direction[0]], axis=0).astype(jnp.bfloat16)
-    coef_table = lax.all_gather(coef_pair, ROW, axis=1, tiled=True)
+    shelf = []
+    for _ in range(lax.axis_size(ROW)):
+        shelf.append(coef_pair)
+    coef_table = jnp.concatenate(lax.all_to_all(jnp.stack(shelf, axis=0), ROW, 0, 0), axis=1)
     nfeat = coef_table.shape[1]
     nblk = nfeat // width
     both = jnp.concatenate([coef, direction], axis=1)

time: 375 us -> 363 us (0.968)
  waiting for transfers between devices: 296 us -> 265 us
  starting transfers between devices: 5.64 us -> 17.1 us
  local copies, waits for them, and re-layouts: 25.5 us -> 34.1 us
    all_gather x1 -> x0, waiting for transfers between devices: 80.7 us -> none  [on_device(): coef_table = lax.all_gather(coef_pair, ROW, axis=1, tiled=True)]
    all_to_all x0 -> x1, waiting for transfers between devices: none -> 49.7 us  [on_device(): lax.all_to_all(jnp.stack(shelf, axis=0), ROW, 0, 0)]
    all_to_all x0 -> x1, starting transfers between devices: none -> 11.5 us  [on_device(): lax.all_to_all(jnp.stack(shelf, axis=0), ROW, 0, 0)]
    another operation x0 -> x3, local copies, waits for them, and re-layouts: none -> 8.72 us  [the longest x2 7.11 us: on_device(): selected = coef_table.reshape(2 * arms, nblk, width)[:, blks]]
where the time goes in v1:
time: 363 us
  waiting for transfers between devices  265 us (73%)
  local copies, waits for them, and re-layouts  34.1 us (9%)
  matrix products  21.1 us (6%)
  starting transfers between devices  17.1 us (5%)
  between operations  14.1 us (4%)
  other arithmetic  10.7 us (3%)
    reduce_scatter x1, waiting for transfers between devices, on_device(): lax.psum_scatter(partial_terms, ROW, scatter_dimension=1, tiled=True)  213 us
    all_to_all x1, waiting for transfers between devices, on_device(): lax.all_to_all(jnp.stack(shelf, axis=0), ROW, 0, 0)  49.7 us
    all_to_all x1, starting transfers between devices, on_device(): lax.all_to_all(jnp.stack(shelf, axis=0), ROW, 0, 0)  11.5 us
    dot_general x1, matrix products, on_device(): jnp.einsum('tari,ktai->tkr', feats, selected, preferred_element_type=jnp....  9.68 us
    dot_general x1, matrix products, on_device(): jnp.einsum('tari,tkr->taki', feats, both_low, preferred_element_type=jnp....  9.02 us
  transfers between devices with their start and end apart: 4, of which 4 were waited for; matrix products, arithmetic and copies ran while one was open for 0% of the time, Pallas kernels for 0%

profile of v1, /device:TPU:4, one launch (start us, length us, event | category | flops | bytes accessed | tf_op | source)
XLA Modules:
  0.0 362.6 jit_solution(11525260892043002913)
XLA Ops:
  7.2 0.0 copy-start
  7.2 0.9 constant_dynamic-update-slice_fusion.1
  8.1 0.9 constant_dynamic-update-slice_fusion
  9.0 1.6 stack.4
  10.7 11.5 %all-to-all-start = ((bf16[32,32,1024]{2,1,0:T(8,128)(2,1)}), bf16[32,32,1024]{2,1,0:T(8,128)(2,1)S(1)}, u32[]{:S(2)}, u32[]{:S(2)}) async-start(bf16[32,32,1024]{2,1,0:T(8,128)(2,1)} %stack.4), calls=%async_computation | async-start | bytes 4194304 | tf_op jit(solution)/shard_map/all_to_all | solution.py:34
  22.2 0.0 reduce-scatter.2.cloned.1.call-start
  22.2 0.0 copy-done
  22.2 0.1 copy.21
  22.3 0.1 copy.17
  22.4 0.1 reshape.95
  22.4 0.1 eq.34
  22.5 49.7 %all-to-all-done = bf16[32,32,1024]{2,1,0:T(8,128)(2,1)S(1)} async-done(((bf16[32,32,1024]{2,1,0:T(8,128)(2,1)}), bf16[32,32,1024]{2,1,0:T(8,128)(2,1)S(1)}, u32[]{:S(2)}, u32[]{:S(2)}) %all-to-all-start) | async-done | bytes 2097184 | tf_op jit(solution)/shard_map/all_to_all | solution.py:34
  72.2 2.5 copy.16
  74.7 4.2 %reshape_reshape.3 = bf16[32,256,128]{2,1,0:T(8,128)(2,1)} reshape(bf16[32,32,1024]{2,1,0:T(8,128)(2,1)} %copy.16) | data formatting | bytes 4194304 | tf_op jit(solution)/shard_map/reshape;reshape | solution.py:40
  78.9 2.9 copy.18
  81.8 3.2 gather_fusion
  85.0 0.0 copy-start.2
  85.0 9.7 %fusion.14 = f32[24,32,128]{2,1,0:T(8,128)S(1)} fusion(bf16[32,24,16,128]{3,0,2,1:T(8,128)(2,1)} %bitcast.55, bf16[1,24,16,128,128]{4,3,2,1,0:T(8,128)(2,1)} %param.6), kind=kOutput, calls=%fused_computation.17 | convolution fusion | flops 402653184 | bytes 16121856 | tf_op jit(solution)/shard_map/tari,ktai->tkr/dot_general | solution.py:42
  94.7 0.0 copy-done.2
  94.7 0.8 subtract_convert_fusion
  95.4 0.1 fusion.20
  95.5 9.0 %fusion.2 = f32[24,32,16,128]{3,1,2,0:T(8,128)} fusion(bf16[1,24,16,128,128]{4,3,2,1,0:T(8,128)(2,1)} %param.6, bf16[24,16,128]{2,1,0:T(8,128)(2,1)S(1)} %fusion.20, bf16[24,16,128]{2,1,0:T(8,128)(2,1)S(1)} %get-tuple-element.10), kind=kOutput, calls=%fused_computation.3 | convolution fusion | flops 403046400 | bytes 19070976 | tf_op jit(solution)/shard_map/tari,tkr->taki/dot_general | solution.py:53
  104.5 6.6 %copy.19 = f32[384,1,32,128]{0,3,2,1:T(8,128)} copy(f32[384,1,32,128]{3,2,0,1:T(8,128)} %bitcast.52) | data formatting | bytes 12582912 | tf_op jit(solution)/shard_map/reshape | solution.py:54
  111.1 4.3 %reduce-precision_convert_fusion = (bf16[384,1,32,128]{0,3,2,1:T(8,128)(2,1)S(1)}, bf16[384,1,32,128]{0,3,2,1:T(8,128)(2,1)S(1)}) fusion(f32[384,1,32,128]{0,3,2,1:T(8,128)} %copy.19), kind=kLoop, calls=%fused_computation.8 | loop fusion | flops 6291456 | bytes 12582912 | tf_op jit(solution)/shard_map/convert_element_type | solution.py:56
  115.4 2.5 fusion.11
  117.8 2.8 slice_add_fusion
  120.6 5.6 %copy.22 = f32[1,32,256,128]{3,2,1,0:T(8,128)} copy(f32[1,32,256,128]{2,3,1,0:T(8,128)} %slice_add_fusion) | data formatting | bytes 8388608 | tf_op jit(solution)/shard_map/add | solution.py:64
  126.1 6.6 %copy.28 = f32[4,8,256,128]{3,1,2,0:T(8,128)} copy(f32[4,8,256,128]{3,2,1,0:T(8,128)} %bitcast.54) | data formatting | bytes 8388608
  132.7 0.0 copy-start.1
  132.7 0.0 reduce-scatter.2.cloned.1.call-update
  132.8 1.9 collective-permute-start
  134.7 3.6 %collective-permute-start.1 = (f32[1,32,1024]{2,1,0:T(8,128)S(1)}, f32[1,32,1024]{2,1,0:T(8,128)S(1)}, u32[]{:S(2)}, u32[]{:S(2)}) collective-permute-start(f32[1,32,1024]{2,1,0:T(8,128)S(1)} %get-tuple-element.6), channel_id=1, source_target_pairs={{32,0},{64,32},{96,64},{128,96},{160,128},{192,160},{224,192},{33,... | collective-permute-start | bytes 393224 | tf_op jit(solution)/shard_map/ppermute | solution.py:20
  138.3 0.7 collective-permute-done
  139.0 1.8 collective-permute-done.1
  140.8 213.3 %reduce-scatter.2.cloned.1.call-done = f32[32,1024]{1,0:T(8,128)} async-done(((f32[32,32768]{1,0:T(8,128)}), f32[32,1024]{1,0:T(8,128)}) %reduce-scatter.2.cloned.1.call-update) | async-done | bytes 131088 | tf_op jit(solution)/shard_map/reduce_scatter | solution.py:66
  354.1 0.0 copy-done.1
  354.1 0.9 fusion.28
  355.0 0.7 slice_bitcast_fusion
  (3 shorter events, 0.0 us)
Async XLA Ops:
  7.2 15.0 %copy-start = (s32[1,24,16]{1,2,0:T(8,128)S(1)}, s32[1,24,16]{1,2,0:T(8,128)}, u32[]{:S(2)}) copy-start(s32[1,24,16]{1,2,0:T(8,128)} %param.7) | copy-start | bytes 4612
  10.7 61.5 %all-to-all-start = ((bf16[32,32,1024]{2,1,0:T(8,128)(2,1)}), bf16[32,32,1024]{2,1,0:T(8,128)(2,1)S(1)}, u32[]{:S(2)}, u32[]{:S(2)}) async-start(bf16[32,32,1024]{2,1,0:T(8,128)(2,1)} %stack.4), calls=%async_computation | async-start | bytes 4194304 | tf_op jit(solution)/shard_map/all_to_all | solution.py:34
  22.2 332.0 %reduce-scatter.2.cloned.1.call-start = ((), (), s32[]{:S(2)}) async-start(), calls=%async_computation.2 | async-start | bytes 4325376 | tf_op jit(solution)/shard_map/reduce_scatter | solution.py:66
  85.0 9.7 %copy-start.2 = (s32[1,24,128]{2,1,0:T(8,128)S(1)}, s32[1,24,128]{2,1,0:T(8,128)}, u32[]{:S(2)}) copy-start(s32[1,24,128]{2,1,0:T(8,128)} %param.8) | copy-start | bytes 36868
  132.7 221.4 %copy-start.1 = (f32[1024]{0:T(1024)S(1)}, f32[1024]{0:T(1024)}, u32[]{:S(2)}) copy-start(f32[1024]{0:T(1024)} %param.11) | copy-start | bytes 12292
  132.8 6.3 %collective-permute-start = (f32[1,32,1024]{2,1,0:T(8,128)S(1)}, f32[1,32,1024]{2,1,0:T(8,128)S(1)}, u32[]{:S(2)}, u32[]{:S(2)}) collective-permute-start(f32[1,32,1024]{2,1,0:T(8,128)S(1)} %get-tuple-element.6), channel_id=1, source_target_pairs={{0,32},{32,64},{64,96},{96,128},{128,160},{160,192},{192,224},{1,3... | collective-permute-start | bytes 393224 | tf_op jit(solution)/shard_map/ppermute | solution.py:18
  134.7 6.1 %collective-permute-start.1 = (f32[1,32,1024]{2,1,0:T(8,128)S(1)}, f32[1,32,1024]{2,1,0:T(8,128)S(1)}, u32[]{:S(2)}, u32[]{:S(2)}) collective-permute-start(f32[1,32,1024]{2,1,0:T(8,128)S(1)} %get-tuple-element.6), channel_id=1, source_target_pairs={{32,0},{64,32},{96,64},{128,96},{160,128},{192,160},{224,192},{33,... | collective-permute-start | bytes 393224 | tf_op jit(solution)/shard_map/ppermute | solution.py:20
Sparse Core Ops, SparseCore 0:
  132.9 221.1 reduce-scatter.1
